TPU v7x, 32 devices: a whole 2x2x4 slice. The times are simulated.
32 devices in a mesh: stream: 2 (over y), dev: 16 (over z, x, core).
Axes of the slice: x: 2, y: 2, z: 4, core: 2. Of those that a mesh axis runs over, the one named last changes fastest.
Arguments:
- latents: bfloat16 [32, 2, 3, 16, 1664], P(('stream', 'dev')), parts along dimension 0, may hold values from -6 to 6
- owners: int32 [4], P('stream'), parts along dimension 0, may hold values from 0 to 15
- conv_in: bfloat16 [432, 384], replicated, may hold values from -0.3125 to 0.3125
- conv_mid: bfloat16 [10368, 384], replicated, may hold values from -0.0625 to 0.0625
- to_pixels: bfloat16 [384, 12], replicated, may hold values from -0.3125 to 0.3125
Outputs:
- pixels: bfloat16 [4, 3, 32, 624], P('stream', None, 'dev'), parts along dimension 0
There are 2 independent parts, one for each index of `stream`. A program takes and returns all parts, laid end to end along the dimension named above; an argument that names none is the same for every part. Nothing has to cross between parts.
Inputs may be any that keep to these rules, and one draw needn't show every extreme that they name: `owners`: each entry is the index of a device on dev.
All inputs are finite; a program needn't handle non-finite values.
Results may differ from a plain program's by a relative error of at most 0.0052.
Values may be sent and summed in bfloat16 or wider, within the bound.
No kernel may reach another device: no remote copies, remote signals or barrier semaphores. Data moves between devices by JAX's collectives and lax.ppermute only.
A program may use at most 128 MiB of HBM per device.

v0:
```python
import jax
import jax.numpy as jnp
from jax import lax
from jax.sharding import PartitionSpec as P

ZC = 16
GROUPS = 2
FRAMES = 3
epsilon = 1e-06


def spread(value, axis, source):
    kept = jnp.where(lax.axis_index(axis) == source, value, 0).astype(value.dtype)
    return lax.psum(kept, axis)


def with_halo(block, sides, width):
    for axis, dim in sides:
        count = lax.axis_size(axis)
        forward = [(i, i + 1) for i in range(count - 1)]
        backward = [(target, source) for source, target in forward]
        low = lax.ppermute(
            lax.slice_in_dim(block, block.shape[dim] - width, None, axis=dim), axis, forward
        )
        high = lax.ppermute(lax.slice_in_dim(block, 0, width, axis=dim), axis, backward)
        block = jnp.concatenate([low, block, high], axis=dim)
    return block


def local_conv(source, weights):
    steps_t = source.shape[0] - 2
    rows_out = source.shape[1] - 2
    columns = source.shape[2]
    channels = source.shape[3]
    padded = jnp.pad(source, ((0, 0), (0, 0), (1, 1), (0, 0)))
    result = jnp.zeros((steps_t * rows_out * columns, weights.shape[1]), jnp.float32)
    for step_t in range(3):
        pieces = []
        for step_r in range(3):
            for step_w in range(3):
                pieces.append(
                    padded[
                        step_t : step_t + steps_t,
                        step_r : step_r + rows_out,
                        step_w : step_w + columns,
                    ]
                )
        stacked = jnp.concatenate(pieces, axis=-1)
        block = weights[step_t * 9 * channels : (step_t + 1) * 9 * channels]
        result = result + jnp.dot(
            stacked.reshape(-1, stacked.shape[-1]), block, preferred_element_type=jnp.float32
        )
    return result.reshape(steps_t, rows_out, columns, weights.shape[1])


def rms_scale(values):
    return values * lax.rsqrt(jnp.mean(values * values, axis=-1, keepdims=True) + epsilon)


def local(latents, owners, conv_in, conv_mid, to_pixels):
    n_devices = lax.axis_size("dev")
    position = lax.axis_index("dev")
    height = latents.shape[3]
    rows_dev = height // n_devices
    columns = latents.shape[4] // ZC
    channels = conv_mid.shape[1]
    first_row = position * rows_dev
    extend = 0
    span_rows = rows_dev + 2 * extend
    latent_cache = jnp.zeros((2, height + 4, columns, ZC), jnp.bfloat16)
    middle_cache = jnp.zeros((2, rows_dev + 2, columns, channels), jnp.bfloat16)
    results = []
    for group in range(GROUPS):
        group_latent = spread(latents[0, group], "dev", owners[group])
        frames = group_latent.reshape(FRAMES, height, columns, ZC)
        frames = jnp.pad(frames, ((0, 0), (2, 2), (0, 0), (0, 0)))
        history = jnp.concatenate([latent_cache, frames], axis=0)
        latent_cache = history[-2:]
        window = lax.dynamic_slice_in_dim(history, first_row + 1 - extend, span_rows + 2, 1)
        first_act = local_conv(window, conv_in)
        activated = jax.nn.silu(rms_scale(first_act)).astype(jnp.bfloat16)
        extended = with_halo(activated, (("dev", 1),), 1)
        middle_history = jnp.concatenate([middle_cache, extended], axis=0)
        middle_cache = middle_history[-2:]
        second_act = local_conv(middle_history, conv_mid)
        normed = rms_scale(first_act + second_act).astype(jnp.bfloat16)
        projected = jnp.dot(
            normed.reshape(-1, channels), to_pixels, preferred_element_type=jnp.float32
        )
        projected = projected.reshape(FRAMES, rows_dev, columns, 2, 2, 3).transpose(
            0, 1, 3, 2, 4, 5
        )
        results.append(projected.reshape(FRAMES, 2 * rows_dev, 6 * columns).astype(jnp.bfloat16))
    return jnp.stack(results, axis=0)


def solution(mesh):
    in_specs = (P(("stream", "dev"), None, None, None, None), P("stream"), P(), P(), P())
    out_specs = P("stream", None, "dev", None)
    return jax.shard_map(local, mesh=mesh, in_specs=in_specs, out_specs=out_specs, check_vma=False)
```

profile of v0, /device:TPU:3, one launch (start us, length us, event | category | flops | bytes accessed | tf_op | source)
XLA Modules:
  0.0 174.3 jit_solution(17543781535209339910)
XLA Ops:
  6.5 1.3 fusion.50
  9.2 1.0 slice_select_fusion
  10.2 2.0 %reshape.290 = bf16[3,16,104,16]{3,2,1,0:T(8,128)(2,1)} reshape(bf16[1,1,3,16,1664]{4,3,2,1,0:T(8,128)(2,1)S(1)} %get-tuple-element.59) | data formatting | bytes 319488 | tf_op jit(solution)/shard_map/reshape | solution.py:75
  12.2 2.0 %reshape.298 = bf16[3,16,104,16]{3,2,1,0:T(8,128)(2,1)} reshape(bf16[1,1,3,16,1664]{4,3,2,1,0:T(8,128)(2,1)S(1)} %get-tuple-element.58) | data formatting | bytes 319488 | tf_op jit(solution)/shard_map/reshape | solution.py:75
  14.2 99.9 %all-reduce.11.cloned.1.call-done = (bf16[3,16,104,16]{3,2,1,0:T(8,128)(2,1)}, bf16[3,16,104,16]{3,2,1,0:T(8,128)(2,1)}) async-done(((bf16[3,16,104,16]{3,2,1,0:T(8,128)(2,1)}, bf16[3,16,104,16]{3,2,1,0:T(8,128)(2,1)}), (bf16[3,16,104,16]{3,2,1,0:T(8,128)(2,1)}, bf16[3,16,104,16]{3,2,1,0:T(8,128)(2,1)})) %all-reduce.11.cloned.1.call-update) | async-done | bytes 319504 | tf_op jit(solution)/shard_map/psum | solution.py:14
  114.1 1.6 pad.23
  116.6 0.4 copy-done.2
  118.0 0.3 multiply_reduce_fusion.3
  118.6 5.2 %collective-permute-start = (bf16[3,1,104,384]{3,2,0,1:T(8,128)(2,1)S(1)}, bf16[3,1,104,384]{3,2,0,1:T(8,128)(2,1)}, u32[]{:S(2)}, u32[]{:S(2)}) collective-permute-start(bf16[3,1,104,384]{3,2,0,1:T(8,128)(2,1)S(1)} %multiply_convert_fusion.5), channel_id=1, source_target_pairs={{0,1},{1,2},{2,3},{3,4},{4,5},{5,6},{6,7},{7,8},{8,9},{9,10},{10,1... | collective-permute-start | bytes 718856 | tf_op jit(solution)/shard_map/ppermute | solution.py:22
  123.8 1.9 %collective-permute-start.1 = (bf16[3,1,104,384]{3,2,0,1:T(8,128)(2,1)S(1)}, bf16[3,1,104,384]{3,2,0,1:T(8,128)(2,1)}, u32[]{:S(2)}, u32[]{:S(2)}) collective-permute-start(bf16[3,1,104,384]{3,2,0,1:T(8,128)(2,1)S(1)} %multiply_convert_fusion.5), channel_id=1, source_target_pairs={{1,0},{2,1},{3,2},{4,3},{5,4},{6,5},{7,6},{8,7},{9,8},{10,9},{11,1... | collective-permute-start | bytes 718856 | tf_op jit(solution)/shard_map/ppermute | solution.py:25
  126.0 0.3 copy.13
  126.3 1.7 copy.21
  130.5 0.4 multiply_reduce_fusion.1
  131.2 4.5 %collective-permute-start.2 = (bf16[3,1,104,384]{3,2,0,1:T(8,128)(2,1)S(1)}, bf16[3,1,104,384]{3,2,0,1:T(8,128)(2,1)S(1)}, u32[]{:S(2)}, u32[]{:S(2)}) collective-permute-start(bf16[3,1,104,384]{3,2,0,1:T(8,128)(2,1)S(1)} %multiply_convert_fusion.2), channel_id=1, source_target_pairs={{0,1},{1,2},{2,3},{3,4},{4,5},{5,6},{6,7},{7,8},{8,9},{9,10},{10,1... | collective-permute-start | bytes 718856 | tf_op jit(solution)/shard_map/ppermute | solution.py:22
  135.8 2.1 %collective-permute-start.3 = (bf16[3,1,104,384]{3,2,0,1:T(8,128)(2,1)S(1)}, bf16[3,1,104,384]{3,2,0,1:T(8,128)(2,1)S(1)}, u32[]{:S(2)}, u32[]{:S(2)}) collective-permute-start(bf16[3,1,104,384]{3,2,0,1:T(8,128)(2,1)S(1)} %multiply_convert_fusion.2), channel_id=1, source_target_pairs={{1,0},{2,1},{3,2},{4,3},{5,4},{6,5},{7,6},{8,7},{9,8},{10,9},{11,1... | collective-permute-start | bytes 718856 | tf_op jit(solution)/shard_map/ppermute | solution.py:25
  137.9 1.2 pad_maximum_fusion
  139.3 0.4 pad_slice_fusion.31
  140.6 1.0 constant_dynamic-update-slice_fusion.6
  142.0 2.2 %collective-permute-done.3 = bf16[3,1,104,384]{3,2,0,1:T(8,128)(2,1)S(1)} collective-permute-done((bf16[3,1,104,384]{3,2,0,1:T(8,128)(2,1)S(1)}, bf16[3,1,104,384]{3,2,0,1:T(8,128)(2,1)S(1)}, u32[]{:S(2)}, u32[]{:S(2)}) %collective-permute-start.3) | collective-permute-done | bytes 239648 | tf_op jit(solution)/shard_map/ppermute | solution.py:25
  144.4 0.4 pad_slice_fusion.25
  145.7 1.1 copy-done.5
  146.9 1.8 %constant_dynamic-update-slice_fusion.1 = bf16[312,3456]{1,0:T(8,128)(2,1)S(1)} fusion(bf16[312,3456]{1,0:T(8,128)(2,1)S(1)} %constant_dynamic-update-slice_fusion.2, bf16[312,384]{1,0:T(8,128)(2,1)} %bitcast.13), kind=kLoop, calls=%fused_computation.95 | loop fusion | bytes 479232
  149.2 1.3 fusion.6
  150.5 1.4 fusion.12
  151.9 1.5 multiply_reduce_fusion.2
  154.0 0.4 convert_element_type.96
  154.8 1.2 copy-done.4
  156.0 3.2 %fusion.4 = f32[312,384]{1,0:T(8,128)S(1)} fusion(bf16[312,3456]{1,0:T(8,128)(2,1)S(1)} %bitcast.98, bf16[10368,384]{1,0:T(8,128)(2,1)} %param.8), kind=kOutput, calls=%fused_computation.14 | convolution fusion | flops 828112896 | bytes 5289984 | tf_op jit(solution)/shard_map/dot_general | solution.py:50
  159.4 3.1 %fusion.15 = f32[312,384]{1,0:T(8,128)S(1)} fusion(f32[312,384]{1,0:T(8,128)S(1)} %fusion.4, bf16[312,3456]{1,0:T(8,128)(2,1)S(1)} %bitcast.100, bf16[10368,384]{1,0:T(8,128)(2,1)} %param.8), kind=kOutput, calls=%fused_computation.28 | convolution fusion | flops 828232704 | bytes 5769216 | tf_op jit(solution)/shard_map/dot_general | solution.py:50
  162.6 3.2 %multiply_reduce_fusion = (f32[312]{0:T(512)S(1)}, f32[312,384]{1,0:T(8,128)S(1)}) fusion(f32[312,384]{1,0:T(8,128)S(1)} %get-tuple-element.72, f32[312,384]{1,0:T(8,128)S(1)} %fusion.15, bf16[312,3456]{1,0:T(8,128)(2,1)S(1)} %constant_dynamic-update-slice_fusion.35, bf16[10368,384]{1,0:T(8,128)(2,1)} %param.8), kind=kOutput, calls=%fused_computation.45 | convolution fusion | flops 828591808 | bytes 6249696 | tf_op jit(solution)/shard_map/dot_general | solution.py:50
  166.4 0.4 convert_element_type.103
  166.8 0.6 pad_maximum_fusion.1
  (126 shorter events, 9.9 us)
Async XLA Ops:
  6.5 107.6 %all-reduce.11.cloned.1.call-start = ((), (), s32[]{:S(2)}) async-start(), calls=%async_computation | async-start | bytes 5111808 | tf_op jit(solution)/shard_map/psum | solution.py:14
  12.2 2.0 %copy-start.7 = (bf16[384,12]{0,1:T(8,128)(2,1)S(1)}, bf16[384,12]{0,1:T(8,128)(2,1)}, u32[]{:S(2)}) copy-start(bf16[384,12]{0,1:T(8,128)(2,1)} %param.9) | copy-start | bytes 27652
  115.9 1.0 copy-start.2
  117.4 8.3 %copy-start.1 = (bf16[3,16,104,16]{3,2,1,0:T(8,128)(2,1)S(1)}, bf16[3,16,104,16]{3,2,1,0:T(8,128)(2,1)}, u32[]{:S(2)}) copy-start(bf16[3,16,104,16]{3,2,1,0:T(8,128)(2,1)} %get-tuple-element.5) | copy-start | bytes 479236
  118.6 19.3 %collective-permute-start = (bf16[3,1,104,384]{3,2,0,1:T(8,128)(2,1)S(1)}, bf16[3,1,104,384]{3,2,0,1:T(8,128)(2,1)}, u32[]{:S(2)}, u32[]{:S(2)}) collective-permute-start(bf16[3,1,104,384]{3,2,0,1:T(8,128)(2,1)S(1)} %multiply_convert_fusion.5), channel_id=1, source_target_pairs={{0,1},{1,2},{2,3},{3,4},{4,5},{5,6},{6,7},{7,8},{8,9},{9,10},{10,1... | collective-permute-start | bytes 718856 | tf_op jit(solution)/shard_map/ppermute | solution.py:22
  123.8 14.1 %collective-permute-start.1 = (bf16[3,1,104,384]{3,2,0,1:T(8,128)(2,1)S(1)}, bf16[3,1,104,384]{3,2,0,1:T(8,128)(2,1)}, u32[]{:S(2)}, u32[]{:S(2)}) collective-permute-start(bf16[3,1,104,384]{3,2,0,1:T(8,128)(2,1)S(1)} %multiply_convert_fusion.5), channel_id=1, source_target_pairs={{1,0},{2,1},{3,2},{4,3},{5,4},{6,5},{7,6},{8,7},{9,8},{10,9},{11,1... | collective-permute-start | bytes 718856 | tf_op jit(solution)/shard_map/ppermute | solution.py:25
  131.2 10.7 %collective-permute-start.2 = (bf16[3,1,104,384]{3,2,0,1:T(8,128)(2,1)S(1)}, bf16[3,1,104,384]{3,2,0,1:T(8,128)(2,1)S(1)}, u32[]{:S(2)}, u32[]{:S(2)}) collective-permute-start(bf16[3,1,104,384]{3,2,0,1:T(8,128)(2,1)S(1)} %multiply_convert_fusion.2), channel_id=1, source_target_pairs={{0,1},{1,2},{2,3},{3,4},{4,5},{5,6},{6,7},{7,8},{8,9},{9,10},{10,1... | collective-permute-start | bytes 718856 | tf_op jit(solution)/shard_map/ppermute | solution.py:22
  135.8 8.3 %collective-permute-start.3 = (bf16[3,1,104,384]{3,2,0,1:T(8,128)(2,1)S(1)}, bf16[3,1,104,384]{3,2,0,1:T(8,128)(2,1)S(1)}, u32[]{:S(2)}, u32[]{:S(2)}) collective-permute-start(bf16[3,1,104,384]{3,2,0,1:T(8,128)(2,1)S(1)} %multiply_convert_fusion.2), channel_id=1, source_target_pairs={{1,0},{2,1},{3,2},{4,3},{5,4},{6,5},{7,6},{8,7},{9,8},{10,9},{11,1... | collective-permute-start | bytes 718856 | tf_op jit(solution)/shard_map/ppermute | solution.py:25
  139.1 1.4 copy-start
  140.6 3.6 %slice-start = ((bf16[3,3,104,384]{3,2,0,1:T(8,128)(2,1)}), bf16[2,3,104,384]{3,2,0,1:T(8,128)(2,1)S(1)}, s32[]{:S(2)}) async-start(bf16[3,3,104,384]{3,2,0,1:T(8,128)(2,1)} %copy-done), calls=%async_computation.1 | async-start | bytes 958464 | tf_op jit(solution)/shard_map/slice | solution.py:84
  145.0 3.9 %slice-start.1 = ((s8[7962624]{0:T(1024)(128)(4,1)}), s8[4194304]{0:T(1024)(128)(4,1)S(1)}, s32[]{:S(2)}) async-start(s8[7962624]{0:T(1024)(128)(4,1)} %bitcast.102), calls=%async_computation.2 | async-start | bytes 8388608
  145.4 1.4 copy-start.5
  145.5 3.7 %slice-start.2 = ((s8[7962624]{0:T(1024)(128)(4,1)}), s8[3768320]{0:T(1024)(128)(4,1)S(1)}, s32[]{:S(2)}) async-start(s8[7962624]{0:T(1024)(128)(4,1)} %bitcast.102), calls=%async_computation.3 | async-start | bytes 7536640
  148.9 1.7 copy-start.3
  154.4 1.6 copy-start.4
  156.0 3.4 %copy-start.6 = (bf16[3,1,104,3456]{3,2,0,1:T(8,128)(2,1)S(1)}, bf16[3,1,104,3456]{3,2,0,1:T(8,128)(2,1)}, u32[]{:S(2)}) copy-start(bf16[3,1,104,3456]{3,2,0,1:T(8,128)(2,1)} %copy-done.5) | copy-start | bytes 6469636
Sparse Core Ops, SparseCore 0:
  14.3 99.7 all-reduce.10
where the time goes:
time: 175 us; the launch traced here: 174 us
  waiting for transfers between devices  102 us (58%)
  local copies, waits for them, and re-layouts  22.8 us (13%)
  matrix products  15.9 us (9%)
  between operations  15.4 us (9%)
  starting transfers between devices  13.8 us (8%)
  other arithmetic  4.23 us (2%)
    psum x1, waiting for transfers between devices, spread(): return lax.psum(kept, axis)  99.9 us
    dot_general x12, matrix products, local_conv(): jnp.dot(stacked.reshape(-1, stacked.shape[-1]), block, preferred_element_...  15.5 us
    unnamed x78, local copies, waits for them, and re-layouts  10.4 us
    ppermute x2, starting transfers between devices, with_halo(): lax.ppermute(lax.slice_in_dim(block, block.shape[dim] - width, None, axis...  9.76 us
    ppermute x2, starting transfers between devices, with_halo(): lax.ppermute(lax.slice_in_dim(block, 0, width, axis=dim), axis, backward)  4.02 us
    reshape x2, local copies, waits for them, and re-layouts, local(): frames = group_latent.reshape(FRAMES, height, columns, ZC)  3.94 us
  transfers between devices with their start and end apart: 5, of which 2 were waited for; matrix products, arithmetic and copies ran while one was open for 5% of the time, Pallas kernels for 0%

commit v1 on v0

--- a/solution.py
+++ b/solution.py
@@ -11,7 +11,7 @@
 
 def spread(value, axis, source):
     kept = jnp.where(lax.axis_index(axis) == source, value, 0).astype(value.dtype)
-    return lax.psum(kept, axis)
+    return jnp.sum(lax.all_gather(kept, axis), axis=0)
 
 
 def with_halo(block, sides, width):

time: 175 us -> 149 us (0.85)
  waiting for transfers between devices: 102 us -> 73 us
  other arithmetic: 4.23 us -> 9.2 us
  starting transfers between devices: 13.8 us -> 11.9 us
    psum x1 -> x0, waiting for transfers between devices: 99.9 us -> none  [spread(): return lax.psum(kept, axis)]
    all_gather x0 -> x2, waiting for transfers between devices: none -> 70.1 us  [spread(): return jnp.sum(lax.all_gather(kept, axis), axis=0)]
    reduce_sum x0 -> x2, other arithmetic: none -> 4.23 us  [spread(): return jnp.sum(lax.all_gather(kept, axis), axis=0)]
    reshape x2, local copies, waits for them, and re-layouts: 3.94 us -> 1.84 us  [local(): frames = group_latent.reshape(FRAMES, height, columns, ZC)]
    concatenate x14, local copies, waits for them, and re-layouts: 1.81 us -> 3.82 us  [local_conv(): stacked = jnp.concatenate(pieces, axis=-1)]
    ppermute x2, starting transfers between devices: 9.76 us -> 7.81 us  [with_halo(): lax.ppermute(lax.slice_in_dim(block, block.shape[dim] - width, None, axis...]
    unnamed x78 -> x76, local copies, waits for them, and re-layouts: 10.4 us -> 8.69 us
  transfers between devices with their start and end apart: 5 -> 6, of which waited for: 2 -> 3; matrix products, arithmetic and copies ran while one was open for 5% -> 15% of each run, Pallas kernels for 0% -> 0%
where the time goes in v1:
time: 149 us; the launch traced here: 148 us
  waiting for transfers between devices  73 us (49%)
  local copies, waits for them, and re-layouts  22.5 us (15%)
  matrix products  15.9 us (11%)
  between operations  15.4 us (10%)
  starting transfers between devices  11.9 us (8%)
  other arithmetic  9.2 us (6%)
    all_gather x2, waiting for transfers between devices, spread(): return jnp.sum(lax.all_gather(kept, axis), axis=0)  70.1 us
    dot_general x12, matrix products, local_conv(): jnp.dot(stacked.reshape(-1, stacked.shape[-1]), block, preferred_element_...  15.5 us
    unnamed x76, local copies, waits for them, and re-layouts  8.69 us
    ppermute x2, starting transfers between devices, with_halo(): lax.ppermute(lax.slice_in_dim(block, block.shape[dim] - width, None, axis...  7.81 us
    reduce_sum x2, other arithmetic, spread(): return jnp.sum(lax.all_gather(kept, axis), axis=0)  4.23 us
    ppermute x2, starting transfers between devices, with_halo(): lax.ppermute(lax.slice_in_dim(block, 0, width, axis=dim), axis, backward)  4.02 us
    concatenate x14, local copies, waits for them, and re-layouts, local_conv(): stacked = jnp.concatenate(pieces, axis=-1)  3.82 us
  transfers between devices with their start and end apart: 6, of which 3 were waited for; matrix products, arithmetic and copies ran while one was open for 15% of the time, Pallas kernels for 0%

profile of v1, /device:TPU:3, one launch (start us, length us, event | category | flops | bytes accessed | tf_op | source)
XLA Modules:
  0.0 148.0 jit_solution(14721160151168851271)
XLA Ops:
  6.5 1.3 fusion.50
  9.2 1.8 %slice_select_fusion = (bf16[1,1,3,16,1664]{4,3,2,1,0:T(8,128)(2,1)}, bf16[1,1,3,16,1664]{4,3,2,1,0:T(8,128)(2,1)}) fusion(bf16[1,2,3,16,1664]{4,3,2,1,0:T(8,128)(2,1)} %param.5, pred[]{:T(512)S(6)} %eq.7, pred[]{:T(512)S(6)} %eq.6), kind=kLoop, calls=%fused_computation.137 | loop fusion | flops 159744 | bytes 638978 | tf_op jit(solution)/shard_map/jit(_where)/select_n | solution.py:13
  11.1 0.7 all-gather.7.cloned.1.call-update
  11.8 0.7 reshape.329
  12.5 42.4 %all-gather.5.cloned.1.call-done = bf16[16,1,3,16,1664]{4,3,2,1,0:T(8,128)(2,1)} async-done(((bf16[1,1,3,16,1664]{4,3,2,1,0:T(8,128)(2,1)}), bf16[16,1,3,16,1664]{4,3,2,1,0:T(8,128)(2,1)}) %all-gather.5.cloned.1.call-update) | async-done | bytes 2555920 | tf_op jit(solution)/shard_map/all_gather | solution.py:14
  54.9 2.1 %reduce_sum.60 = bf16[3,16,1664]{2,1,0:T(8,128)(2,1)S(1)} reduce(bf16[16,1,3,16,1664]{4,3,2,1,0:T(8,128)(2,1)} %all-gather.5.cloned.1.call-done, bf16[]{:T(256)} %constant.23.clone.1), dimensions={0,1}, to_apply=%region_0.1 | reduce | flops 1198080 | bytes 2715650 | tf_op jit(solution)/shard_map/reduce_sum | solution.py:14
  57.0 0.9 reshape.310
  58.5 0.9 pad_slice_fusion.8
  59.4 0.9 pad_dynamic-slice_fusion
  60.2 1.4 concatenate.91
  61.6 1.2 concatenate.90
  64.2 3.9 %collective-permute-start = (bf16[3,1,104,384]{3,2,0,1:T(8,128)(2,1)S(1)}, bf16[3,1,104,384]{3,2,0,1:T(8,128)(2,1)}, u32[]{:S(2)}, u32[]{:S(2)}) collective-permute-start(bf16[3,1,104,384]{3,2,0,1:T(8,128)(2,1)S(1)} %multiply_convert_fusion.5), channel_id=1, source_target_pairs={{0,1},{1,2},{2,3},{3,4},{4,5},{5,6},{6,7},{7,8},{8,9},{9,10},{10,1... | collective-permute-start | bytes 718856 | tf_op jit(solution)/shard_map/ppermute | solution.py:22
  68.1 1.9 %collective-permute-start.1 = (bf16[3,1,104,384]{3,2,0,1:T(8,128)(2,1)S(1)}, bf16[3,1,104,384]{3,2,0,1:T(8,128)(2,1)}, u32[]{:S(2)}, u32[]{:S(2)}) collective-permute-start(bf16[3,1,104,384]{3,2,0,1:T(8,128)(2,1)S(1)} %multiply_convert_fusion.5), channel_id=1, source_target_pairs={{1,0},{2,1},{3,2},{4,3},{5,4},{6,5},{7,6},{8,7},{9,8},{10,9},{11,1... | collective-permute-start | bytes 718856 | tf_op jit(solution)/shard_map/ppermute | solution.py:25
  70.2 1.0 copy.13
  71.2 27.7 %all-gather.7.cloned.1.call-done = bf16[16,1,3,16,1664]{4,3,2,1,0:T(8,128)(2,1)} async-done(((bf16[1,1,3,16,1664]{4,3,2,1,0:T(8,128)(2,1)}), bf16[16,1,3,16,1664]{4,3,2,1,0:T(8,128)(2,1)}) %all-gather.7.cloned.1.call-update) | async-done | bytes 2555920 | tf_op jit(solution)/shard_map/all_gather | solution.py:14
  98.9 2.1 %reduce_sum.63 = bf16[3,16,1664]{2,1,0:T(8,128)(2,1)S(1)} reduce(bf16[16,1,3,16,1664]{4,3,2,1,0:T(8,128)(2,1)} %all-gather.7.cloned.1.call-done, bf16[]{:T(256)} %constant.23.clone.1), dimensions={0,1}, to_apply=%region_3.4 | reduce | flops 1198080 | bytes 2715650 | tf_op jit(solution)/shard_map/reduce_sum | solution.py:14
  101.1 0.9 reshape.318
  105.6 3.9 %collective-permute-start.2 = (bf16[3,1,104,384]{3,2,0,1:T(8,128)(2,1)S(1)}, bf16[3,1,104,384]{3,2,0,1:T(8,128)(2,1)S(1)}, u32[]{:S(2)}, u32[]{:S(2)}) collective-permute-start(bf16[3,1,104,384]{3,2,0,1:T(8,128)(2,1)S(1)} %multiply_convert_fusion.2), channel_id=1, source_target_pairs={{0,1},{1,2},{2,3},{3,4},{4,5},{5,6},{6,7},{7,8},{8,9},{9,10},{10,1... | collective-permute-start | bytes 718856 | tf_op jit(solution)/shard_map/ppermute | solution.py:22
  109.5 2.1 %collective-permute-start.3 = (bf16[3,1,104,384]{3,2,0,1:T(8,128)(2,1)S(1)}, bf16[3,1,104,384]{3,2,0,1:T(8,128)(2,1)S(1)}, u32[]{:S(2)}, u32[]{:S(2)}) collective-permute-start(bf16[3,1,104,384]{3,2,0,1:T(8,128)(2,1)S(1)} %multiply_convert_fusion.2), channel_id=1, source_target_pairs={{1,0},{2,1},{3,2},{4,3},{5,4},{6,5},{7,6},{8,7},{9,8},{10,9},{11,1... | collective-permute-start | bytes 718856 | tf_op jit(solution)/shard_map/ppermute | solution.py:25
  111.6 1.2 pad_maximum_fusion
  114.3 1.0 constant_dynamic-update-slice_fusion.6
  115.7 2.2 %collective-permute-done.3 = bf16[3,1,104,384]{3,2,0,1:T(8,128)(2,1)S(1)} collective-permute-done((bf16[3,1,104,384]{3,2,0,1:T(8,128)(2,1)S(1)}, bf16[3,1,104,384]{3,2,0,1:T(8,128)(2,1)S(1)}, u32[]{:S(2)}, u32[]{:S(2)}) %collective-permute-start.3) | collective-permute-done | bytes 239648 | tf_op jit(solution)/shard_map/ppermute | solution.py:25
  119.4 1.1 copy-done.5
  120.6 1.8 %constant_dynamic-update-slice_fusion.1 = bf16[312,3456]{1,0:T(8,128)(2,1)S(1)} fusion(bf16[312,3456]{1,0:T(8,128)(2,1)S(1)} %constant_dynamic-update-slice_fusion.2, bf16[312,384]{1,0:T(8,128)(2,1)} %bitcast.13), kind=kLoop, calls=%fused_computation.95 | loop fusion | bytes 479232
  122.9 1.3 fusion.6
  124.3 1.4 fusion.12
  125.7 1.5 %multiply_reduce_fusion.2 = (f32[312]{0:T(512)S(1)}, f32[312,384]{1,0:T(8,128)S(1)}) fusion(f32[312,384]{1,0:T(8,128)S(1)} %get-tuple-element.72, f32[312,384]{1,0:T(8,128)S(1)} %fusion.12, bf16[312,3456]{1,0:T(8,128)(2,1)S(1)} %constant_dynamic-update-slice_fusion, bf16[10368,384]{1,0:T(8,128)(2,1)S(1)} %bitcast.99), kind=kOutput, calls=%fused_computation.50 | convolution fusion | flops 828591808 | bytes 6249696 | tf_op jit(solution)/shard_map/dot_general | solution.py:50
  128.5 1.2 copy-done.4
  129.7 3.2 %fusion.4 = f32[312,384]{1,0:T(8,128)S(1)} fusion(bf16[312,3456]{1,0:T(8,128)(2,1)S(1)} %bitcast.94, bf16[10368,384]{1,0:T(8,128)(2,1)} %param.8), kind=kOutput, calls=%fused_computation.14 | convolution fusion | flops 828112896 | bytes 5289984 | tf_op jit(solution)/shard_map/dot_general | solution.py:50
  133.2 3.1 %fusion.15 = f32[312,384]{1,0:T(8,128)S(1)} fusion(f32[312,384]{1,0:T(8,128)S(1)} %fusion.4, bf16[312,3456]{1,0:T(8,128)(2,1)S(1)} %bitcast.96, bf16[10368,384]{1,0:T(8,128)(2,1)} %param.8), kind=kOutput, calls=%fused_computation.28 | convolution fusion | flops 828232704 | bytes 5769216 | tf_op jit(solution)/shard_map/dot_general | solution.py:50
  136.3 3.2 %multiply_reduce_fusion = (f32[312]{0:T(512)S(1)}, f32[312,384]{1,0:T(8,128)S(1)}) fusion(f32[312,384]{1,0:T(8,128)S(1)} %get-tuple-element.70, f32[312,384]{1,0:T(8,128)S(1)} %fusion.15, bf16[312,3456]{1,0:T(8,128)(2,1)S(1)} %constant_dynamic-update-slice_fusion.35, bf16[10368,384]{1,0:T(8,128)(2,1)} %param.8), kind=kOutput, calls=%fused_computation.45 | convolution fusion | flops 828591808 | bytes 6249696 | tf_op jit(solution)/shard_map/dot_general | solution.py:50
  140.5 0.6 pad_maximum_fusion.1
  (129 shorter events, 12.0 us)
Async XLA Ops:
  6.5 48.4 %all-gather.5.cloned.1.call-start = ((), (), s32[]{:S(2)}) async-start(), calls=%async_computation | async-start | bytes 2715648 | tf_op jit(solution)/shard_map/all_gather | solution.py:14
  11.0 87.9 %all-gather.7.cloned.1.call-start = ((), (), s32[]{:S(2)}) async-start(), calls=%async_computation.1 | async-start | bytes 2715648 | tf_op jit(solution)/shard_map/all_gather | solution.py:14
  59.4 3.7 %copy-start.1 = (bf16[432,384]{1,0:T(8,128)(2,1)S(1)}, bf16[432,384]{1,0:T(8,128)(2,1)}, u32[]{:S(2)}) copy-start(bf16[432,384]{1,0:T(8,128)(2,1)} %param.7) | copy-start | bytes 995332
  64.2 47.4 %collective-permute-start = (bf16[3,1,104,384]{3,2,0,1:T(8,128)(2,1)S(1)}, bf16[3,1,104,384]{3,2,0,1:T(8,128)(2,1)}, u32[]{:S(2)}, u32[]{:S(2)}) collective-permute-start(bf16[3,1,104,384]{3,2,0,1:T(8,128)(2,1)S(1)} %multiply_convert_fusion.5), channel_id=1, source_target_pairs={{0,1},{1,2},{2,3},{3,4},{4,5},{5,6},{6,7},{7,8},{8,9},{9,10},{10,1... | collective-permute-start | bytes 718856 | tf_op jit(solution)/shard_map/ppermute | solution.py:22
  68.1 43.5 %collective-permute-start.1 = (bf16[3,1,104,384]{3,2,0,1:T(8,128)(2,1)S(1)}, bf16[3,1,104,384]{3,2,0,1:T(8,128)(2,1)}, u32[]{:S(2)}, u32[]{:S(2)}) collective-permute-start(bf16[3,1,104,384]{3,2,0,1:T(8,128)(2,1)S(1)} %multiply_convert_fusion.5), channel_id=1, source_target_pairs={{1,0},{2,1},{3,2},{4,3},{5,4},{6,5},{7,6},{8,7},{9,8},{10,9},{11,1... | collective-permute-start | bytes 718856 | tf_op jit(solution)/shard_map/ppermute | solution.py:25
  71.2 31.2 %copy-start.2 = (bf16[2,20,104,16]{2,3,1,0:T(8,128)(2,1)S(1)}, bf16[2,20,104,16]{2,3,1,0:T(8,128)(2,1)}, u32[]{:S(2)}) copy-start(bf16[2,20,104,16]{2,3,1,0:T(8,128)(2,1)} %copy.13) | copy-start | bytes 399364
  105.6 10.1 %collective-permute-start.2 = (bf16[3,1,104,384]{3,2,0,1:T(8,128)(2,1)S(1)}, bf16[3,1,104,384]{3,2,0,1:T(8,128)(2,1)S(1)}, u32[]{:S(2)}, u32[]{:S(2)}) collective-permute-start(bf16[3,1,104,384]{3,2,0,1:T(8,128)(2,1)S(1)} %multiply_convert_fusion.2), channel_id=1, source_target_pairs={{0,1},{1,2},{2,3},{3,4},{4,5},{5,6},{6,7},{7,8},{8,9},{9,10},{10,1... | collective-permute-start | bytes 718856 | tf_op jit(solution)/shard_map/ppermute | solution.py:22
  109.5 8.3 %collective-permute-start.3 = (bf16[3,1,104,384]{3,2,0,1:T(8,128)(2,1)S(1)}, bf16[3,1,104,384]{3,2,0,1:T(8,128)(2,1)S(1)}, u32[]{:S(2)}, u32[]{:S(2)}) collective-permute-start(bf16[3,1,104,384]{3,2,0,1:T(8,128)(2,1)S(1)} %multiply_convert_fusion.2), channel_id=1, source_target_pairs={{1,0},{2,1},{3,2},{4,3},{5,4},{6,5},{7,6},{8,7},{9,8},{10,9},{11,1... | collective-permute-start | bytes 718856 | tf_op jit(solution)/shard_map/ppermute | solution.py:25
  112.8 1.4 copy-start
  114.3 3.6 %slice-start = ((bf16[3,3,104,384]{3,2,0,1:T(8,128)(2,1)}), bf16[2,3,104,384]{3,2,0,1:T(8,128)(2,1)S(1)}, s32[]{:S(2)}) async-start(bf16[3,3,104,384]{3,2,0,1:T(8,128)(2,1)} %copy-done), calls=%async_computation.2 | async-start | bytes 958464 | tf_op jit(solution)/shard_map/slice | solution.py:84
  118.7 3.9 %slice-start.1 = ((s8[7962624]{0:T(1024)(128)(4,1)}), s8[4194304]{0:T(1024)(128)(4,1)S(1)}, s32[]{:S(2)}) async-start(s8[7962624]{0:T(1024)(128)(4,1)} %bitcast.98), calls=%async_computation.3 | async-start | bytes 8388608
  119.1 1.4 copy-start.5
  119.3 3.7 %slice-start.2 = ((s8[7962624]{0:T(1024)(128)(4,1)}), s8[3768320]{0:T(1024)(128)(4,1)S(1)}, s32[]{:S(2)}) async-start(s8[7962624]{0:T(1024)(128)(4,1)} %bitcast.98), calls=%async_computation.4 | async-start | bytes 7536640
  122.6 1.7 %copy-start.3 = (bf16[3,1,104,3456]{3,2,0,1:T(8,128)(2,1)}, bf16[3,1,104,3456]{3,2,0,1:T(8,128)(2,1)S(1)}, u32[]{:S(2)}) copy-start(bf16[3,1,104,3456]{3,2,0,1:T(8,128)(2,1)S(1)} %get-tuple-element.77) | copy-start | bytes 6469636
  128.1 1.6 %copy-start.4 = (bf16[3,1,104,3456]{3,2,0,1:T(8,128)(2,1)S(1)}, bf16[3,1,104,3456]{3,2,0,1:T(8,128)(2,1)}, u32[]{:S(2)}) copy-start(bf16[3,1,104,3456]{3,2,0,1:T(8,128)(2,1)} %copy-done.3) | copy-start | bytes 6469636
  129.7 3.4 %copy-start.6 = (bf16[3,1,104,3456]{3,2,0,1:T(8,128)(2,1)S(1)}, bf16[3,1,104,3456]{3,2,0,1:T(8,128)(2,1)}, u32[]{:S(2)}) copy-start(bf16[3,1,104,3456]{3,2,0,1:T(8,128)(2,1)} %copy-done.5) | copy-start | bytes 6469636
Sparse Core Ops, SparseCore 0:
  11.1 43.7 all-gather.4
  57.1 41.8 all-gather.6
